TPU v7x, 256 devices: a whole 4x4x8 slice. The times are simulated.
256 devices in a mesh: agent: 4 (over y), tile: 64 (over x, z, core).
Axes of the slice: x: 4, y: 4, z: 8, core: 2. Of those that a mesh axis runs over, the one named last changes fastest.
Arguments:
- feats: bfloat16 [32, 256, 24, 256], P('agent', 'tile'), may hold values from -18 to 18
- types: int32 [32], replicated, may hold values from 0 to 1
- valid: int32 [32], replicated, may hold values 0 or 1
- offsets: int32 [32, 2], replicated, may hold values from -2 to 2
- w_qkv: bfloat16 [2, 256, 768], replicated, may hold values from -0.375 to 0.375
- w_out: bfloat16 [2, 256, 256], replicated, may hold values from -0.375 to 0.375
- d_out: bfloat16 [32, 256, 24, 256], P('agent', 'tile'), may hold values from -6 to 6
Outputs:
- d_feats: bfloat16 [32, 256, 24, 256], P('agent', 'tile')
- g_qkv: float32 [2, 256, 768], P(None, 'tile')
- g_out: float32 [2, 256, 256], P(None, 'tile')
All inputs are finite; a program needn't handle non-finite values.
Results may differ from a plain program's by a relative error of at most 0.012.
The roundings to bfloat16 on the way count: a program that leaves them out, or rounds other values in their place, can miss the bound.
Values may be sent and summed in bfloat16 or wider, within the bound.
No kernel may reach another device: no remote copies, remote signals or barrier semaphores. Data moves between devices by JAX's collectives and lax.ppermute only.
A program may use at most 128 MiB of HBM per device.

v0:
```python
import math
import jax
import jax.numpy as jnp
from jax import lax
from jax.sharding import PartitionSpec as P

HEADS = 8
MAXOFF = 2


def axis_bits(axis):
    count = lax.axis_size(axis)
    bits = count.bit_length() - 1
    assert 1 << bits == count
    return bits


def xor_pairs(count, bit):
    return [(i, i ^ 1 << bit) for i in range(count)]


def tile_bit_order(count):
    bits = count.bit_length() - 1
    preferred = [0, 1, 4, 2, 5, 3]
    return [b for b in preferred if b < bits] + [b for b in range(bits) if b not in preferred]


def halving_sum(pieces, axis, bit_order):
    count = lax.axis_size(axis)
    me = lax.axis_index(axis)
    bits = axis_bits(axis)
    rest = pieces.shape[1:]
    x = pieces.reshape((2,) * bits + rest)
    for bit in bit_order:
        dim = bits - 1 - bit
        mine = me >> bit & 1
        low = lax.index_in_dim(x, 0, dim, keepdims=True)
        high = lax.index_in_dim(x, 1, dim, keepdims=True)
        keep = jnp.where(mine == 1, high, low)
        send = jnp.where(mine == 1, low, high)
        x = keep + lax.ppermute(send, axis, xor_pairs(count, bit))
    return x.reshape(rest)


def doubling_sum(x, axis, bit_order):
    count = lax.axis_size(axis)
    for bit in bit_order:
        x = x + lax.ppermute(x, axis, xor_pairs(count, bit))
    return x


def with_halo(cells, sides, width):
    for axis, dim in sides:
        count = lax.axis_size(axis)
        ends = count - 1
        head = lax.slice_in_dim(cells, 0, width, axis=dim)
        tail = lax.slice_in_dim(cells, cells.shape[dim] - width, cells.shape[dim], axis=dim)
        cells = jnp.concatenate(
            [
                lax.ppermute(tail, axis, [(i, (i + 1) % count) for i in range(ends)]),
                cells,
                lax.ppermute(head, axis, [((i + 1) % count, i) for i in range(ends)]),
            ],
            axis=dim,
        )
    return cells


def relocate(rimmed, offsets, direction):
    padded = jnp.pad(rimmed, ((0, 0), (0, 0), (MAXOFF, MAXOFF), (0, 0)))
    row_count = rimmed.shape[1] - 2 * MAXOFF
    col_count = rimmed.shape[2]

    def pick_one(plane, offset):
        row_start = MAXOFF + direction * offset[0]
        col_start = MAXOFF + direction * offset[1]
        return lax.dynamic_slice(
            plane, (row_start, col_start, jnp.int32(0)), (row_count, col_count, plane.shape[2])
        )

    return jax.vmap(pick_one)(padded, offsets)


def body(feats, types, valid, offsets, w_qkv, w_out, d_out):
    f32 = jnp.float32
    bf16 = jnp.bfloat16
    highest = lax.Precision.HIGHEST
    own_count, row_count, col_count, channels = feats.shape
    agents = own_count * lax.axis_size("agent")
    first_agent = lax.axis_index("agent") * own_count
    own_offsets = lax.dynamic_slice_in_dim(offsets, first_agent, own_count, 0)
    rimmed = with_halo(feats, (("tile", 1),), MAXOFF)
    warped = relocate(rimmed, own_offsets, 1)
    cell_count = row_count * col_count
    head_size = channels // HEADS
    score_scale = head_size ** (-0.5)
    all_hot = (types[:, None] == jnp.arange(2)[None, :]).astype(bf16)
    flat_feats = warped.reshape(own_count, cell_count, channels)
    flat_grads = d_out.reshape(own_count, cell_count, channels)
    all_feats, all_grads = (
        lax.all_to_all(flat_feats, "agent", split_axis=1, concat_axis=0, tiled=True),
        lax.all_to_all(flat_grads, "agent", split_axis=1, concat_axis=0, tiled=True),
    )
    part_cells = all_feats.shape[1]
    pairs = agents * part_cells
    is_type1 = (types == 1)[:, None, None]
    type_mask = jnp.stack([types == 0, types == 1], axis=0)[:, :, None, None]
    feats_rows = all_feats.reshape(pairs, channels)
    grads_rows = all_grads.reshape(pairs, channels)
    qkv_both = (
        jnp.einsum("pc,tce->tpe", feats_rows, w_qkv, preferred_element_type=f32)
        .astype(bf16)
        .reshape(2, agents, part_cells, 3 * channels)
    )
    qkv = jnp.where(is_type1, qkv_both[1], qkv_both[0])
    query_heads = qkv[..., :channels].reshape(agents, part_cells, HEADS, head_size)
    key_heads = qkv[..., channels : 2 * channels].reshape(agents, part_cells, HEADS, head_size)
    value_heads = qkv[..., 2 * channels :].reshape(agents, part_cells, HEADS, head_size)
    scores = (
        jnp.einsum("aghd,bghd->ghab", query_heads, key_heads, preferred_element_type=f32)
        * score_scale
    )
    agent_ids = jnp.arange(agents)
    allowed = (valid[None, :] == 1) | (agent_ids[:, None] == agent_ids[None, :])
    raised = jnp.where(allowed, jnp.exp(scores), f32(0.0))
    attn_prob = raised / jnp.sum(raised, axis=-1, keepdims=True)
    prob_low = attn_prob.astype(bf16)
    attended = (
        jnp.einsum("ghab,bghd->aghd", prob_low, value_heads, preferred_element_type=f32)
        .astype(bf16)
        .reshape(agents, part_cells, channels)
    )
    d_att_both = (
        jnp.einsum("pe,tce->tpc", grads_rows, w_out, preferred_element_type=f32)
        .astype(bf16)
        .reshape(2, agents, part_cells, channels)
    )
    d_attended = jnp.where(is_type1, d_att_both[1], d_att_both[0])
    attended_typed = jnp.where(type_mask, attended[None], jnp.zeros((), bf16))
    raw_out = jnp.einsum(
        "tpc,pe->tce",
        attended_typed.reshape(2, pairs, channels),
        grads_rows,
        preferred_element_type=f32,
    )
    attended_heads = d_attended.reshape(agents, part_cells, HEADS, head_size)
    prob_grad = jnp.einsum(
        "aghd,bghd->ghab", attended_heads, value_heads, preferred_element_type=f32
    )
    score_grad = (
        attn_prob
        * (prob_grad - jnp.sum(attn_prob * prob_grad, axis=-1, keepdims=True))
        * score_scale
    ).astype(bf16)
    d_query = (
        jnp.einsum("ghab,bghd->aghd", score_grad, key_heads, preferred_element_type=f32)
        .astype(bf16)
        .reshape(agents, part_cells, channels)
    )
    groups_n = agents // own_count
    grad_blocks = score_grad.reshape(part_cells, HEADS, groups_n, own_count, agents)
    prob_blocks = prob_low.reshape(part_cells, HEADS, groups_n, own_count, agents)
    query_blocks = query_heads.reshape(groups_n, own_count, part_cells, HEADS, head_size)
    dattn_blocks = attended_heads.reshape(groups_n, own_count, part_cells, HEADS, head_size)
    key_parts = jnp.einsum(
        "ghnyb,nyghd->nbghd", grad_blocks, query_blocks, preferred_element_type=f32
    ).astype(bf16)
    value_parts = jnp.einsum(
        "ghnyb,nyghd->nbghd", prob_blocks, dattn_blocks, preferred_element_type=f32
    ).astype(bf16)
    key_sum = jnp.sum(key_parts.astype(f32), axis=0).reshape(agents, part_cells, channels)
    value_sum = jnp.sum(value_parts.astype(f32), axis=0).reshape(agents, part_cells, channels)
    d_qkv = jnp.concatenate([d_query.astype(f32), key_sum, value_sum], axis=-1)
    d_hi = d_qkv.astype(bf16)
    d_lo = (d_qkv - d_hi.astype(f32)).astype(bf16)
    d_split = jnp.stack([d_hi, d_lo], axis=0).reshape(2, pairs, 3 * channels)
    d_part_terms = jnp.einsum("spe,tce->stpc", d_split, w_qkv, preferred_element_type=f32)
    d_part_sum = (d_part_terms[0] + d_part_terms[1]).reshape(2, agents, part_cells, channels)
    d_part = jnp.where(is_type1, d_part_sum[1], d_part_sum[0]).astype(bf16)
    returned = lax.all_to_all(d_part, "agent", split_axis=0, concat_axis=1, tiled=True)
    d_warped = returned.reshape(own_count, row_count, col_count, channels)
    feats_typed = jnp.where(type_mask, all_feats[None], jnp.zeros((), bf16)).reshape(
        2, pairs, channels
    )
    qkv_terms = jnp.einsum("tpc,spe->stce", feats_typed, d_split, preferred_element_type=f32)
    raw_qkv = qkv_terms[0] + qkv_terms[1]
    rimmed_grad = with_halo(d_warped, (("tile", 1),), MAXOFF)
    d_feats = relocate(rimmed_grad, own_offsets, -1)
    norm_limit = math.sqrt(8.0 * channels * channels)
    raw_all = jnp.concatenate([raw_qkv, raw_out], axis=-1)
    tiles = lax.axis_size("tile")
    share_rows = channels // tiles
    pieces = raw_all.reshape(2, tiles, share_rows, 4 * channels).transpose(1, 0, 2, 3)
    share_all = halving_sum(pieces, "tile", tile_bit_order(tiles))
    share_all = doubling_sum(share_all, "agent", list(range(axis_bits("agent"))))
    square_sum = jnp.broadcast_to(jnp.sum(share_all * share_all), (8, 128))
    square_sum = doubling_sum(square_sum, "tile", list(range(axis_bits("tile"))))[0, 0]
    factor = norm_limit / jnp.maximum(jnp.sqrt(square_sum), norm_limit)
    scaled = share_all * factor
    return (d_feats, scaled[..., : 3 * channels], scaled[..., 3 * channels :])


def solution(mesh):
    placed = (
        P("agent", "tile", None, None),
        P(),
        P(),
        P(),
        P(),
        P(),
        P("agent", "tile", None, None),
    )
    return jax.shard_map(
        body,
        mesh=mesh,
        in_specs=placed,
        out_specs=(P("agent", "tile", None, None), P(None, "tile", None), P(None, "tile", None)),
        check_vma=False,
    )
```

profile of v0, /device:TPU:2, one launch (start us, length us, event | category | flops | bytes accessed | tf_op | source)
XLA Modules:
  0.0 232.1 jit_solution(8492455447294959551)
XLA Ops:
  0.7 2.0 copy.109
  2.7 4.5 %all-to-all-start.1 = ((bf16[8,96,256]{2,0,1:T(8,128)(2,1)}), bf16[8,96,256]{2,0,1:T(8,128)(2,1)S(1)}, u32[]{:S(2)}, u32[]{:S(2)}) async-start(bf16[8,96,256]{2,0,1:T(8,128)(2,1)} %bitcast.10), calls=%async_computation.1 | async-start | bytes 786432 | tf_op jit(solution)/shard_map/all_to_all | solution.py:102
  7.2 1.2 copy.102
  8.4 1.9 collective-permute-start
  10.4 6.9 %collective-permute-start.1 = (bf16[8,2,24,256]{3,0,2,1:T(8,128)(2,1)S(1)}, bf16[8,2,24,256]{3,0,2,1:T(8,128)(2,1)S(1)}, u32[]{:S(2)}, u32[]{:S(2)}) collective-permute-start(bf16[8,2,24,256]{3,0,2,1:T(8,128)(2,1)S(1)} %get-tuple-element.33), channel_id=1, source_target_pairs={{1,0},{2,1},{3,2},{4,3},{5,4},{6,5},{7,6},{8,7},{9,8},{10,9},{11,1... | collective-permute-start | bytes 589832 | tf_op jit(solution)/shard_map/ppermute | solution.py:62
  18.7 1.8 collective-permute-done.1
  20.5 2.4 %gather_fusion = bf16[8,4,24,256]{3,0,2,1:T(8,128)(2,1)} fusion(bf16[8,8,28,256]{3,0,2,1:T(8,128)(2,1)S(1)} %fusion.32, s32[8]{0:T(128)S(1)} %get-tuple-element.35), kind=kCustom, calls=%fused_computation | custom fusion | bytes 786560 | tf_op jit(solution)/shard_map/vmap()/gather | solution.py:77
  23.0 5.0 %all-to-all-start = ((bf16[8,96,256]{2,0,1:T(8,128)(2,1)}), bf16[8,96,256]{2,0,1:T(8,128)(2,1)S(1)}, u32[]{:S(2)}, u32[]{:S(2)}) async-start(bf16[8,96,256]{2,0,1:T(8,128)(2,1)} %bitcast.1), calls=%async_computation | async-start | bytes 786432 | tf_op jit(solution)/shard_map/all_to_all | solution.py:101
  29.7 1.8 squeeze.33
  31.6 1.8 squeeze.36
  33.5 1.8 squeeze.34
  35.3 3.4 %broadcast_select_fusion = bf16[32,24,8,32]{3,2,1,0:T(8,128)(2,1)} fusion(bf16[32,24,8,32]{3,2,1,0:T(8,128)(2,1)} %squeeze.33, bf16[32,24,8,32]{3,2,1,0:T(8,128)(2,1)} %squeeze.34, pred[32]{0:T(512)(128)(4,1)S(1)} %get-tuple-element.38), kind=kLoop, calls=%fused_computation.44 | loop fusion | flops 196608 | bytes 1179680 | tf_op jit(solution)/shard_map/jit(_where)/select_n | solution.py:138
  38.7 1.4 broadcast_select_fusion.1
  41.4 1.8 reshape_reshape.4
  43.2 1.8 reshape.321
  45.0 1.6 copy.158
  47.6 3.8 %fusion.3 = (f32[24,8,32]{2,1,0:T(8,128)S(1)}, f32[24,8,32,32]{2,3,1,0:T(8,128)S(1)}) fusion(pred[32,32]{0,1:T(8,128)(4,1)S(1)} %fusion.44, bf16[32,24,8,32]{0,3,2,1:T(8,128)(2,1)S(1)} %bitcast.136, bf16[32,24,8,32]{3,2,1,0:T(8,128)(2,1)} %reshape.321), kind=kOutput, calls=%fused_computation.12 | convolution fusion | flops 13166592 | bytes 1598464 | tf_op jit(solution)/shard_map/aghd,bghd->ghab/dot_general | solution.py:120
  51.4 1.6 copy-done.5
  53.8 1.7 copy.125
  55.6 3.3 %fusion.26 = bf16[32,24,8,32]{0,3,2,1:T(8,128)(2,1)} fusion(bf16[32,24,8,32]{0,3,2,1:T(8,128)(2,1)} %bitcast.116, bf16[24,8,32,32]{2,3,1,0:T(8,128)(2,1)S(1)} %fusion.59), kind=kOutput, calls=%fused_computation.46 | convolution fusion | flops 12779520 | bytes 1179648 | tf_op jit(solution)/shard_map/ghab,bghd->aghd/dot_general | solution.py:129
  58.9 2.9 %fusion.22 = f32[24,8,32,32]{2,3,1,0:T(8,128)} fusion(bf16[32,24,8,32]{0,3,2,1:T(8,128)(2,1)S(1)} %bitcast.117, bf16[32,24,8,32]{3,2,1,0:T(8,128)(2,1)S(1)} %copy-done.3), kind=kOutput, calls=%fused_computation.40 | convolution fusion | flops 12582912 | bytes 1572864 | tf_op jit(solution)/shard_map/aghd,bghd->ghab/dot_general | solution.py:147
  61.8 8.2 %fusion.15 = f32[24,8,32,32]{3,2,1,0:T(8,128)} fusion(bf16[32,24,8,32]{0,3,2,1:T(8,128)(2,1)S(1)} %bitcast.137, f32[24,8,32,32]{2,3,1,0:T(8,128)} %fusion.22, f32[24,8,32,32]{2,3,1,0:T(8,128)} %copy-done.5, f32[24,8,32]{2,1,0:T(8,128)S(1)} %get-tuple-element.39, pred[32,32]{0,1:T(8,128)(4,1)S(1)} %fusion.44), kind=kOutput, calls=%fused_computation.31 | convolution fusion | flops 15144991 | bytes 2778112 | tf_op jit(solution)/shard_map/ghab,bghd->aghd/dot_general | solution.py:156
  70.0 6.7 %multiply_convert_fusion = bf16[24,8,32,32]{2,3,1,0:T(8,128)(2,1)S(1)} fusion(f32[24,8,32,32]{2,3,1,0:T(8,128)} %fusion.22, f32[24,8,32]{2,1,0:T(8,128)} %copy-done.16, f32[24,8,32,32]{2,3,1,0:T(8,128)} %copy-done.5, pred[32,32]{0,1:T(8,128)(4,1)S(1)} %fusion.44), kind=kOutput, calls=%fused_computation.5 | output fusion | flops 2168863 | bytes 1991680 | tf_op jit(solution)/shard_map/sub | solution.py:152
  76.8 4.5 %convert_reduce_fusion = f32[24,8,32,32]{3,2,1,0:T(8,128)} fusion(bf16[4,8,24,8,32]{4,3,2,1,0:T(8,128)(2,1)S(1)} %copy-done.7, bf16[24,8,32,32]{3,2,1,0:T(8,128)(2,1)S(1)} %copy-done.8), kind=kOutput, calls=%fused_computation.3 | convolution fusion | flops 14745600 | bytes 1572864 | tf_op jit(solution)/shard_map/ghnyb,nyghd->nbghd/dot_general | solution.py:168
  81.3 2.3 copy.152
  83.6 1.6 copy.119
  85.2 2.3 copy.132
  87.5 6.2 %convert_reduce_fusion.1 = f32[24,8,32,32]{3,2,1,0:T(8,128)} fusion(bf16[4,8,24,8,32]{4,3,2,1,0:T(8,128)(2,1)} %reshape_reshape.4, bf16[24,8,32,32]{3,2,1,0:T(8,128)(2,1)} %copy.119), kind=kOutput, calls=%fused_computation.4 | convolution fusion | flops 14745600 | bytes 1572864 | tf_op jit(solution)/shard_map/ghnyb,nyghd->nbghd/dot_general | solution.py:165
  93.7 2.3 copy.151
  96.0 1.2 subtract_convert_fusion
  99.3 3.8 %copy.137 = bf16[32,24,8,32]{3,2,1,0:T(8,128)(2,1)S(1)} copy(bf16[32,24,8,32]{0,3,2,1:T(8,128)(2,1)} %fusion.26) | data formatting | bytes 786432 | tf_op jit(solution)/shard_map/convert_element_type | solution.py:130
  103.0 1.8 broadcast_in_dim.106
  104.9 2.8 %fusion.12 = f32[2,2,256,768]{2,3,1,0:T(8,128)S(1)} fusion(bf16[1,32,24,768]{3,1,2,0:T(8,128)(2,1)S(1)} %copy-done.13, bf16[1,32,24,768]{3,1,2,0:T(8,128)(2,1)} %fusion.16, pred[2,32]{1,0:T(4,128)(4,1)S(1)} %copy-done.20, bf16[32,24,256]{2,0,1:T(8,128)(2,1)} %copy.134), kind=kOutput, calls=%fused_computation.26 | convolution fusion | flops 1213071360 | bytes 5898304 | tf_op jit(solution)/shard_map/tpc,spe->stce/dot_general | solution.py:185
  109.6 2.4 %copy.139 = f32[2,256,1024]{2,0,1:T(2,128)} copy(f32[2,256,1024]{1,2,0:T(8,128)S(1)} %pad_maximum_fusion.1) | data formatting | bytes 4194304 | tf_op jit(solution)/shard_map/concatenate | solution.py:190
  112.0 2.4 %fusion.62 = (f32[2,2,2,2,2,1,2,4,1024]{8,6,7,5,4,3,2,1,0:T(2,128)S(1)}, f32[2,2,2,2,2,1,2,4,1024]{8,6,7,5,4,3,2,1,0:T(2,128)S(1)}) fusion(f32[2,2,2,2,2,2,2,4,1024]{8,6,7,5,4,3,2,1,0:T(2,128)} %bitcast.124), kind=kLoop, calls=%fused_computation.114 | loop fusion | bytes 4194304 | tf_op jit(solution)/shard_map/slice | solution.py:38
  116.4 2.8 %collective-permute-done.4 = f32[2,2,2,2,2,1,2,4,1024]{8,7,6,5,4,3,2,1,0:T(4,128)} collective-permute-done((f32[2,2,2,2,2,1,2,4,1024]{8,7,6,5,4,3,2,1,0:T(4,128)S(1)}, f32[2,2,2,2,2,1,2,4,1024]{8,7,6,5,4,3,2,1,0:T(4,128)}, u32[]{:S(2)}, u32[]{:S(2)}) %collective-permute-start.4) | collective-permute-done | bytes 1048608 | tf_op jit(solution)/shard_map/ppermute | solution.py:41
  119.2 2.6 %select_add_fusion = f32[2,2,2,2,2,1,2,4,1024]{8,7,6,5,4,3,2,1,0:T(4,128)S(1)} fusion(f32[2,2,2,2,2,1,2,4,1024]{8,7,6,5,4,3,2,1,0:T(4,128)} %collective-permute-done.4, f32[2,2,2,2,2,1,2,4,1024]{8,6,7,5,4,3,2,1,0:T(2,128)} %copy-done.2, f32[2,2,2,2,2,1,2,4,1024]{8,6,7,5,4,3,2,1,0:T(2,128)S(1)} %get-tuple-element.21, pred[]{:T(512)S(6)} %eq.62), kind=kLoop, calls=%fused_computation.50 | loop fusion | flops 524288 | bytes 4194305 | tf_op jit(solution)/shard_map/add | solution.py:41
  123.2 5.2 %copy.118 = f32[32,24,8,32]{3,2,1,0:T(8,128)} copy(f32[32,24,8,32]{0,3,2,1:T(8,128)} %bitcast.121) | data formatting | bytes 1572864 | tf_op jit(solution)/shard_map/concatenate | solution.py:173
  128.4 2.4 %reshape.330 = f32[1,768,256]{2,1,0:T(8,128)S(1)} reshape(f32[32,24,8,32]{3,2,1,0:T(8,128)} %copy.118) | data formatting | bytes 1572864 | tf_op jit(solution)/shard_map/concatenate | solution.py:173
  130.8 4.8 %copy.122 = f32[32,24,8,32]{3,2,1,0:T(8,128)} copy(f32[32,24,8,32]{0,3,2,1:T(8,128)} %bitcast.123) | data formatting | bytes 1572864 | tf_op jit(solution)/shard_map/reduce_sum | solution.py:171
  135.6 2.4 %concatenate.75 = f32[1,768,256]{2,1,0:T(8,128)S(1)} reshape(f32[32,24,8,32]{3,2,1,0:T(8,128)} %copy.122) | data formatting | bytes 1572864 | tf_op jit(solution)/shard_map/concatenate | solution.py:173
  138.0 4.8 %copy.128 = f32[32,24,8,32]{3,2,1,0:T(8,128)} copy(f32[32,24,8,32]{0,3,2,1:T(8,128)} %bitcast.119) | data formatting | bytes 1572864 | tf_op jit(solution)/shard_map/reduce_sum | solution.py:172
  142.8 3.1 %concatenate.76 = f32[1,768,256]{2,1,0:T(8,128)} reshape(f32[32,24,8,32]{3,2,1,0:T(8,128)} %copy.128) | data formatting | bytes 1572864 | tf_op jit(solution)/shard_map/concatenate | solution.py:173
  147.1 1.3 select_add_fusion.1
  149.4 7.5 %collective-permute-done.6 = f32[2,1,2,2,1,1,2,4,1024]{8,7,6,5,4,3,2,1,0:T(4,128)S(1)} collective-permute-done((f32[2,1,2,2,1,1,2,4,1024]{8,7,6,5,4,3,2,1,0:T(4,128)S(1)}, f32[2,1,2,2,1,1,2,4,1024]{8,7,6,5,4,3,2,1,0:T(4,128)S(1)}, u32[]{:S(2)}, u32[]{:S(2)}) %collective-permute-start.6) | collective-permute-done | bytes 262176 | tf_op jit(solution)/shard_map/ppermute | solution.py:41
  157.0 5.8 %collective-permute-start.7 = (f32[2,1,2,1,1,1,2,4,1024]{8,7,6,5,4,3,2,1,0:T(4,128)S(1)}, f32[2,1,2,1,1,1,2,4,1024]{8,7,6,5,4,3,2,1,0:T(4,128)S(1)}, u32[]{:S(2)}, u32[]{:S(2)}) collective-permute-start(f32[2,1,2,1,1,1,2,4,1024]{8,7,6,5,4,3,2,1,0:T(4,128)S(1)} %slice_select_fusion.2), channel_id=1, source_target_pairs={{0,4},{1,5},{2,6},{3,7},{4,0},{5,1},{6,2},{7,3},{8,12},{9,13},{10,... | collective-permute-start | bytes 393224 | tf_op jit(solution)/shard_map/ppermute | solution.py:41
  162.8 1.4 fusion.13
  164.2 4.3 %collective-permute-done.7 = f32[2,1,2,1,1,1,2,4,1024]{8,7,6,5,4,3,2,1,0:T(4,128)S(1)} collective-permute-done((f32[2,1,2,1,1,1,2,4,1024]{8,7,6,5,4,3,2,1,0:T(4,128)S(1)}, f32[2,1,2,1,1,1,2,4,1024]{8,7,6,5,4,3,2,1,0:T(4,128)S(1)}, u32[]{:S(2)}, u32[]{:S(2)}) %collective-permute-start.7) | collective-permute-done | bytes 131104 | tf_op jit(solution)/shard_map/ppermute | solution.py:41
  168.6 2.2 collective-permute-start.8
  171.0 3.5 %collective-permute-done.8 = f32[1,1,2,1,1,1,2,4,1024]{8,7,6,5,4,3,2,1,0:T(4,128)S(1)} collective-permute-done((f32[1,1,2,1,1,1,2,4,1024]{8,7,6,5,4,3,2,1,0:T(4,128)S(1)}, f32[1,1,2,1,1,1,2,4,1024]{8,7,6,5,4,3,2,1,0:T(4,128)S(1)}, u32[]{:S(2)}, u32[]{:S(2)}) %collective-permute-start.8) | collective-permute-done | bytes 65568 | tf_op jit(solution)/shard_map/ppermute | solution.py:41
  174.5 2.4 %collective-permute-start.9 = (f32[1,1,1,1,1,1,2,4,1024]{8,7,6,5,4,3,2,1,0:T(4,128)S(1)}, f32[1,1,1,1,1,1,2,4,1024]{8,7,6,5,4,3,2,1,0:T(4,128)S(1)}, u32[]{:S(2)}, u32[]{:S(2)}) collective-permute-start(f32[1,1,1,1,1,1,2,4,1024]{8,7,6,5,4,3,2,1,0:T(4,128)S(1)} %slice_select_fusion.4), channel_id=1, source_target_pairs={{0,8},{1,9},{2,10},{3,11},{4,12},{5,13},{6,14},{7,15},{8,0},{9,1},... | collective-permute-start | bytes 98312 | tf_op jit(solution)/shard_map/ppermute | solution.py:41
  177.0 5.4 %collective-permute-done.9 = f32[1,1,1,1,1,1,2,4,1024]{8,7,6,5,4,3,2,1,0:T(4,128)S(1)} collective-permute-done((f32[1,1,1,1,1,1,2,4,1024]{8,7,6,5,4,3,2,1,0:T(4,128)S(1)}, f32[1,1,1,1,1,1,2,4,1024]{8,7,6,5,4,3,2,1,0:T(4,128)S(1)}, u32[]{:S(2)}, u32[]{:S(2)}) %collective-permute-start.9) | collective-permute-done | bytes 32800 | tf_op jit(solution)/shard_map/ppermute | solution.py:41
  182.4 1.8 collective-permute-start.10
  185.1 3.9 %all-to-all-start.2 = ((bf16[32,24,256]{2,1,0:T(8,128)(2,1)}), bf16[32,24,256]{2,1,0:T(8,128)(2,1)S(1)}, u32[]{:S(2)}, u32[]{:S(2)}) async-start(bf16[32,24,256]{2,1,0:T(8,128)(2,1)} %select_convert_fusion), calls=%async_computation.2 | async-start | bytes 786432 | tf_op jit(solution)/shard_map/all_to_all | solution.py:180
  189.1 3.6 %collective-permute-start.11 = (f32[2,4,1024]{2,1,0:T(4,128)S(1)}, f32[2,4,1024]{2,1,0:T(4,128)S(1)}, u32[]{:S(2)}, u32[]{:S(2)}) collective-permute-start(f32[2,4,1024]{2,1,0:T(4,128)S(1)} %add.123), channel_id=1, source_target_pairs={{0,128},{64,192},{128,0},{192,64},{1,129},{65,193},{129,1},{193,65... | collective-permute-start | bytes 98312 | tf_op jit(solution)/shard_map/ppermute | solution.py:48
  192.7 4.1 %collective-permute-done.11 = f32[2,4,1024]{2,1,0:T(4,128)S(1)} collective-permute-done((f32[2,4,1024]{2,1,0:T(4,128)S(1)}, f32[2,4,1024]{2,1,0:T(4,128)S(1)}, u32[]{:S(2)}, u32[]{:S(2)}) %collective-permute-start.11) | collective-permute-done | bytes 32800 | tf_op jit(solution)/shard_map/ppermute | solution.py:48
  200.3 2.1 collective-permute-start.2
  202.3 5.6 %collective-permute-start.3 = (bf16[8,2,24,256]{3,0,2,1:T(8,128)(2,1)S(1)}, bf16[8,2,24,256]{3,0,2,1:T(8,128)(2,1)S(1)}, u32[]{:S(2)}, u32[]{:S(2)}) collective-permute-start(bf16[8,2,24,256]{3,0,2,1:T(8,128)(2,1)S(1)} %get-tuple-element.31), channel_id=1, source_target_pairs={{1,0},{2,1},{3,2},{4,3},{5,4},{6,5},{7,6},{8,7},{9,8},{10,9},{11,1... | collective-permute-start | bytes 589832 | tf_op jit(solution)/shard_map/ppermute | solution.py:62
  209.8 3.4 %collective-permute-done.14 = f32[8,128]{1,0:T(8,128)S(1)} collective-permute-done((f32[8,128]{1,0:T(8,128)S(1)}, f32[8,128]{1,0:T(8,128)S(1)}, u32[]{:S(2)}, u32[]{:S(2)}) %collective-permute-start.14) | collective-permute-done | bytes 4128 | tf_op jit(solution)/shard_map/ppermute | solution.py:48
  213.2 1.4 collective-permute-start.15
  214.7 6.1 %collective-permute-done.15 = f32[8,128]{1,0:T(8,128)S(1)} collective-permute-done((f32[8,128]{1,0:T(8,128)S(1)}, f32[8,128]{1,0:T(8,128)S(1)}, u32[]{:S(2)}, u32[]{:S(2)}) %collective-permute-start.15) | collective-permute-done | bytes 4128 | tf_op jit(solution)/shard_map/ppermute | solution.py:48
  220.9 3.5 %collective-permute-done.16 = f32[8,128]{1,0:T(8,128)S(1)} collective-permute-done((f32[8,128]{1,0:T(8,128)S(1)}, f32[8,128]{1,0:T(8,128)S(1)}, u32[]{:S(2)}, u32[]{:S(2)}) %collective-permute-start.16) | collective-permute-done | bytes 4128 | tf_op jit(solution)/shard_map/ppermute | solution.py:48
  224.4 2.1 collective-permute-start.17
  226.6 1.7 gather_fusion.1
  (126 shorter events, 25.5 us)
Async XLA Ops:
  0.6 39.5 %copy-start = (bf16[2,256,768]{2,1,0:T(8,128)(2,1)S(1)}, bf16[2,256,768]{2,1,0:T(8,128)(2,1)}, u32[]{:S(2)}) copy-start(bf16[2,256,768]{2,1,0:T(8,128)(2,1)} %param.11) | copy-start | bytes 2359300
  0.6 16.6 %copy-start.22 = (s32[32]{0:T(128)S(1)}, s32[32]{0:T(128)}, u32[]{:S(2)}) copy-start(s32[32]{0:T(128)} %param.9) | copy-start | bytes 388
  0.7 16.6 %copy-start.21 = (s32[32]{0:T(128)S(1)}, s32[32]{0:T(128)}, u32[]{:S(2)}) copy-start(s32[32]{0:T(128)} %param.8) | copy-start | bytes 388
  0.7 17.5 %copy-start.17 = (s32[32,2]{0,1:T(2,128)S(1)}, s32[32,2]{0,1:T(2,128)}, u32[]{:S(2)}) copy-start(s32[32,2]{0,1:T(2,128)} %param.10) | copy-start | bytes 772
  2.7 20.2 %all-to-all-start.1 = ((bf16[8,96,256]{2,0,1:T(8,128)(2,1)}), bf16[8,96,256]{2,0,1:T(8,128)(2,1)S(1)}, u32[]{:S(2)}, u32[]{:S(2)}) async-start(bf16[8,96,256]{2,0,1:T(8,128)(2,1)} %bitcast.10), calls=%async_computation.1 | async-start | bytes 786432 | tf_op jit(solution)/shard_map/all_to_all | solution.py:102
  8.4 10.2 %collective-permute-start = (bf16[8,2,24,256]{3,0,2,1:T(8,128)(2,1)S(1)}, bf16[8,2,24,256]{3,0,2,1:T(8,128)(2,1)S(1)}, u32[]{:S(2)}, u32[]{:S(2)}) collective-permute-start(bf16[8,2,24,256]{3,0,2,1:T(8,128)(2,1)S(1)} %get-tuple-element.32), channel_id=1, source_target_pairs={{0,1},{1,2},{2,3},{3,4},{4,5},{5,6},{6,7},{7,8},{8,9},{9,10},{10,1... | collective-permute-start | bytes 589832 | tf_op jit(solution)/shard_map/ppermute | solution.py:60
  10.4 10.1 %collective-permute-start.1 = (bf16[8,2,24,256]{3,0,2,1:T(8,128)(2,1)S(1)}, bf16[8,2,24,256]{3,0,2,1:T(8,128)(2,1)S(1)}, u32[]{:S(2)}, u32[]{:S(2)}) collective-permute-start(bf16[8,2,24,256]{3,0,2,1:T(8,128)(2,1)S(1)} %get-tuple-element.33), channel_id=1, source_target_pairs={{1,0},{2,1},{3,2},{4,3},{5,4},{6,5},{7,6},{8,7},{9,8},{10,9},{11,1... | collective-permute-start | bytes 589832 | tf_op jit(solution)/shard_map/ppermute | solution.py:62
  18.0 0.7 copy-start.19
  20.5 7.6 %copy-start.15 = (bf16[2,256,256]{2,1,0:T(8,128)(2,1)S(1)}, bf16[2,256,256]{2,1,0:T(8,128)(2,1)}, u32[]{:S(2)}) copy-start(bf16[2,256,256]{2,1,0:T(8,128)(2,1)} %param.12) | copy-start | bytes 786436
  23.0 17.1 %all-to-all-start = ((bf16[8,96,256]{2,0,1:T(8,128)(2,1)}), bf16[8,96,256]{2,0,1:T(8,128)(2,1)S(1)}, u32[]{:S(2)}, u32[]{:S(2)}) async-start(bf16[8,96,256]{2,0,1:T(8,128)(2,1)} %bitcast.1), calls=%async_computation | async-start | bytes 786432 | tf_op jit(solution)/shard_map/all_to_all | solution.py:101
  28.1 0.8 copy-start.9
  35.2 3.4 %copy-start.4 = (bf16[4,8,24,8,32]{4,3,2,1,0:T(8,128)(2,1)S(1)}, bf16[4,8,24,8,32]{4,3,2,1,0:T(8,128)(2,1)}, u32[]{:S(2)}) copy-start(bf16[4,8,24,8,32]{4,3,2,1,0:T(8,128)(2,1)} %squeeze.36) | copy-start | bytes 1179652
  35.2 3.4 %copy-start.18 = (pred[4,8]{1,0:T(4,128)(4,1)S(1)}, pred[4,8]{1,0:T(4,128)(4,1)}, u32[]{:S(2)}) copy-start(pred[4,8]{1,0:T(4,128)(4,1)} %broadcast_in_dim.97) | copy-start | bytes 100
  47.5 3.8 %copy-start.11 = (bf16[32,24,256]{0,2,1:T(8,128)(2,1)}, bf16[32,24,256]{0,2,1:T(8,128)(2,1)S(1)}, u32[]{:S(2)}) copy-start(bf16[32,24,256]{0,2,1:T(8,128)(2,1)S(1)} %copy.157) | copy-start | bytes 1179652
  51.4 1.6 copy-start.5
  51.4 10.4 %copy-start.16 = (f32[24,8,32]{2,1,0:T(8,128)}, f32[24,8,32]{2,1,0:T(8,128)S(1)}, u32[]{:S(2)}) copy-start(f32[24,8,32]{2,1,0:T(8,128)S(1)} %get-tuple-element.39) | copy-start | bytes 73732
  55.6 3.3 %copy-start.1 = (bf16[32,24,256]{0,2,1:T(8,128)(2,1)S(1)}, bf16[32,24,256]{0,2,1:T(8,128)(2,1)}, u32[]{:S(2)}) copy-start(bf16[32,24,256]{0,2,1:T(8,128)(2,1)} %copy.158) | copy-start | bytes 1179652
  55.6 3.3 %copy-start.3 = (bf16[32,24,8,32]{3,2,1,0:T(8,128)(2,1)S(1)}, bf16[32,24,8,32]{3,2,1,0:T(8,128)(2,1)}, u32[]{:S(2)}) copy-start(bf16[32,24,8,32]{3,2,1,0:T(8,128)(2,1)} %broadcast_select_fusion) | copy-start | bytes 1179652
  58.9 2.9 %copy-start.12 = (bf16[32,24,256]{0,2,1:T(8,128)(2,1)S(1)}, bf16[32,24,256]{0,2,1:T(8,128)(2,1)}, u32[]{:S(2)}) copy-start(bf16[32,24,256]{0,2,1:T(8,128)(2,1)} %copy-done.11) | copy-start | bytes 1179652
  70.0 6.7 %copy-start.7 = (bf16[4,8,24,8,32]{4,3,2,1,0:T(8,128)(2,1)S(1)}, bf16[4,8,24,8,32]{4,3,2,1,0:T(8,128)(2,1)}, u32[]{:S(2)}) copy-start(bf16[4,8,24,8,32]{4,3,2,1,0:T(8,128)(2,1)} %broadcast_select_fusion.1) | copy-start | bytes 1179652
  70.0 6.7 %copy-start.8 = (bf16[24,8,32,32]{3,2,1,0:T(8,128)(2,1)S(1)}, bf16[24,8,32,32]{3,2,1,0:T(8,128)(2,1)}, u32[]{:S(2)}) copy-start(bf16[24,8,32,32]{3,2,1,0:T(8,128)(2,1)} %copy.125) | copy-start | bytes 1179652
  99.2 5.7 %copy-start.13 = (bf16[1,32,24,768]{3,1,2,0:T(8,128)(2,1)S(1)}, bf16[1,32,24,768]{3,1,2,0:T(8,128)(2,1)}, u32[]{:S(2)}) copy-start(bf16[1,32,24,768]{3,1,2,0:T(8,128)(2,1)} %subtract_convert_fusion) | copy-start | bytes 3538948
  99.3 5.7 %copy-start.20 = (pred[2,32]{1,0:T(4,128)(4,1)S(1)}, pred[2,32]{1,0:T(4,128)(4,1)}, u32[]{:S(2)}) copy-start(pred[2,32]{1,0:T(4,128)(4,1)} %copy-done.19) | copy-start | bytes 196
  107.7 1.0 copy-start.10
  107.8 1.1 copy-start.14
  114.4 1.0 copy-start.2
  116.3 2.9 %collective-permute-start.4 = (f32[2,2,2,2,2,1,2,4,1024]{8,7,6,5,4,3,2,1,0:T(4,128)S(1)}, f32[2,2,2,2,2,1,2,4,1024]{8,7,6,5,4,3,2,1,0:T(4,128)}, u32[]{:S(2)}, u32[]{:S(2)}) collective-permute-start(f32[2,2,2,2,2,1,2,4,1024]{8,7,6,5,4,3,2,1,0:T(4,128)S(1)} %copy_select_fusion), channel_id=1, source_target_pairs={{0,1},{1,0},{2,3},{3,2},{4,5},{5,4},{6,7},{7,6},{8,9},{9,8},{10,11... | collective-permute-start | bytes 3145736 | tf_op jit(solution)/shard_map/ppermute | solution.py:41
  122.7 24.3 %collective-permute-start.5 = (f32[2,2,2,2,1,1,2,4,1024]{8,7,6,5,4,3,2,1,0:T(4,128)}, f32[2,2,2,2,1,1,2,4,1024]{8,7,6,5,4,3,2,1,0:T(4,128)}, u32[]{:S(2)}, u32[]{:S(2)}) collective-permute-start(f32[2,2,2,2,1,1,2,4,1024]{8,7,6,5,4,3,2,1,0:T(4,128)} %slice_select_fusion), channel_id=1, source_target_pairs={{0,2},{1,3},{2,0},{3,1},{4,6},{5,7},{6,4},{7,5},{8,10},{9,11},{10,... | collective-permute-start | bytes 1572872 | tf_op jit(solution)/shard_map/ppermute | solution.py:41
  145.9 1.1 copy-start.6
  148.5 8.4 %collective-permute-start.6 = (f32[2,1,2,2,1,1,2,4,1024]{8,7,6,5,4,3,2,1,0:T(4,128)S(1)}, f32[2,1,2,2,1,1,2,4,1024]{8,7,6,5,4,3,2,1,0:T(4,128)S(1)}, u32[]{:S(2)}, u32[]{:S(2)}) collective-permute-start(f32[2,1,2,2,1,1,2,4,1024]{8,7,6,5,4,3,2,1,0:T(4,128)S(1)} %slice_select_fusion.1), channel_id=1, source_target_pairs={{0,16},{1,17},{2,18},{3,19},{4,20},{5,21},{6,22},{7,23},{8,24},{9,... | collective-permute-start | bytes 786440 | tf_op jit(solution)/shard_map/ppermute | solution.py:41
  157.0 11.5 %collective-permute-start.7 = (f32[2,1,2,1,1,1,2,4,1024]{8,7,6,5,4,3,2,1,0:T(4,128)S(1)}, f32[2,1,2,1,1,1,2,4,1024]{8,7,6,5,4,3,2,1,0:T(4,128)S(1)}, u32[]{:S(2)}, u32[]{:S(2)}) collective-permute-start(f32[2,1,2,1,1,1,2,4,1024]{8,7,6,5,4,3,2,1,0:T(4,128)S(1)} %slice_select_fusion.2), channel_id=1, source_target_pairs={{0,4},{1,5},{2,6},{3,7},{4,0},{5,1},{6,2},{7,3},{8,12},{9,13},{10,... | collective-permute-start | bytes 393224 | tf_op jit(solution)/shard_map/ppermute | solution.py:41
  168.6 5.9 %collective-permute-start.8 = (f32[1,1,2,1,1,1,2,4,1024]{8,7,6,5,4,3,2,1,0:T(4,128)S(1)}, f32[1,1,2,1,1,1,2,4,1024]{8,7,6,5,4,3,2,1,0:T(4,128)S(1)}, u32[]{:S(2)}, u32[]{:S(2)}) collective-permute-start(f32[1,1,2,1,1,1,2,4,1024]{8,7,6,5,4,3,2,1,0:T(4,128)S(1)} %slice_select_fusion.3), channel_id=1, source_target_pairs={{0,32},{1,33},{2,34},{3,35},{4,36},{5,37},{6,38},{7,39},{8,40},{9,... | collective-permute-start | bytes 196616 | tf_op jit(solution)/shard_map/ppermute | solution.py:41
  174.5 7.9 %collective-permute-start.9 = (f32[1,1,1,1,1,1,2,4,1024]{8,7,6,5,4,3,2,1,0:T(4,128)S(1)}, f32[1,1,1,1,1,1,2,4,1024]{8,7,6,5,4,3,2,1,0:T(4,128)S(1)}, u32[]{:S(2)}, u32[]{:S(2)}) collective-permute-start(f32[1,1,1,1,1,1,2,4,1024]{8,7,6,5,4,3,2,1,0:T(4,128)S(1)} %slice_select_fusion.4), channel_id=1, source_target_pairs={{0,8},{1,9},{2,10},{3,11},{4,12},{5,13},{6,14},{7,15},{8,0},{9,1},... | collective-permute-start | bytes 98312 | tf_op jit(solution)/shard_map/ppermute | solution.py:41
  182.4 6.6 %collective-permute-start.10 = (f32[2,4,1024]{2,1,0:T(4,128)S(1)}, f32[2,4,1024]{2,1,0:T(4,128)S(1)}, u32[]{:S(2)}, u32[]{:S(2)}) collective-permute-start(f32[2,4,1024]{2,1,0:T(4,128)S(1)} %add_bitcast_fusion), channel_id=1, source_target_pairs={{0,64},{64,0},{128,192},{192,128},{1,65},{65,1},{129,193},{193,129... | collective-permute-start | bytes 98312 | tf_op jit(solution)/shard_map/ppermute | solution.py:48
  185.1 13.2 %all-to-all-start.2 = ((bf16[32,24,256]{2,1,0:T(8,128)(2,1)}), bf16[32,24,256]{2,1,0:T(8,128)(2,1)S(1)}, u32[]{:S(2)}, u32[]{:S(2)}) async-start(bf16[32,24,256]{2,1,0:T(8,128)(2,1)} %select_convert_fusion), calls=%async_computation.2 | async-start | bytes 786432 | tf_op jit(solution)/shard_map/all_to_all | solution.py:180
  189.1 7.7 %collective-permute-start.11 = (f32[2,4,1024]{2,1,0:T(4,128)S(1)}, f32[2,4,1024]{2,1,0:T(4,128)S(1)}, u32[]{:S(2)}, u32[]{:S(2)}) collective-permute-start(f32[2,4,1024]{2,1,0:T(4,128)S(1)} %add.123), channel_id=1, source_target_pairs={{0,128},{64,192},{128,0},{192,64},{1,129},{65,193},{129,1},{193,65... | collective-permute-start | bytes 98312 | tf_op jit(solution)/shard_map/ppermute | solution.py:48
  198.0 1.4 collective-permute-start.12
  200.1 7.8 %collective-permute-start.13 = (f32[8,128]{1,0:T(8,128)S(1)}, f32[8,128]{1,0:T(8,128)S(1)}, u32[]{:S(2)}, u32[]{:S(2)}) collective-permute-start(f32[8,128]{1,0:T(8,128)S(1)} %broadcast_add_fusion), channel_id=1, source_target_pairs={{0,2},{1,3},{2,0},{3,1},{4,6},{5,7},{6,4},{7,5},{8,10},{9,11},{10,... | collective-permute-start | bytes 12296 | tf_op jit(solution)/shard_map/ppermute | solution.py:48
  200.3 26.2 %collective-permute-start.2 = (bf16[8,2,24,256]{3,0,2,1:T(8,128)(2,1)S(1)}, bf16[8,2,24,256]{3,0,2,1:T(8,128)(2,1)S(1)}, u32[]{:S(2)}, u32[]{:S(2)}) collective-permute-start(bf16[8,2,24,256]{3,0,2,1:T(8,128)(2,1)S(1)} %get-tuple-element.30), channel_id=1, source_target_pairs={{0,1},{1,2},{2,3},{3,4},{4,5},{5,6},{6,7},{7,8},{8,9},{9,10},{10,1... | collective-permute-start | bytes 589832 | tf_op jit(solution)/shard_map/ppermute | solution.py:60
  202.3 24.1 %collective-permute-start.3 = (bf16[8,2,24,256]{3,0,2,1:T(8,128)(2,1)S(1)}, bf16[8,2,24,256]{3,0,2,1:T(8,128)(2,1)S(1)}, u32[]{:S(2)}, u32[]{:S(2)}) collective-permute-start(bf16[8,2,24,256]{3,0,2,1:T(8,128)(2,1)S(1)} %get-tuple-element.31), channel_id=1, source_target_pairs={{1,0},{2,1},{3,2},{4,3},{5,4},{6,5},{7,6},{8,7},{9,8},{10,9},{11,1... | collective-permute-start | bytes 589832 | tf_op jit(solution)/shard_map/ppermute | solution.py:62
  208.6 4.6 %collective-permute-start.14 = (f32[8,128]{1,0:T(8,128)S(1)}, f32[8,128]{1,0:T(8,128)S(1)}, u32[]{:S(2)}, u32[]{:S(2)}) collective-permute-start(f32[8,128]{1,0:T(8,128)S(1)} %fusion.78), channel_id=1, source_target_pairs={{0,4},{1,5},{2,6},{3,7},{4,0},{5,1},{6,2},{7,3},{8,12},{9,13},{10,... | collective-permute-start | bytes 12296 | tf_op jit(solution)/shard_map/ppermute | solution.py:48
  213.2 7.5 %collective-permute-start.15 = (f32[8,128]{1,0:T(8,128)S(1)}, f32[8,128]{1,0:T(8,128)S(1)}, u32[]{:S(2)}, u32[]{:S(2)}) collective-permute-start(f32[8,128]{1,0:T(8,128)S(1)} %add.127), channel_id=1, source_target_pairs={{0,8},{1,9},{2,10},{3,11},{4,12},{5,13},{6,14},{7,15},{8,0},{9,1},... | collective-permute-start | bytes 12296 | tf_op jit(solution)/shard_map/ppermute | solution.py:48
  220.7 3.6 %collective-permute-start.16 = (f32[8,128]{1,0:T(8,128)S(1)}, f32[8,128]{1,0:T(8,128)S(1)}, u32[]{:S(2)}, u32[]{:S(2)}) collective-permute-start(f32[8,128]{1,0:T(8,128)S(1)} %add.128), channel_id=1, source_target_pairs={{0,16},{1,17},{2,18},{3,19},{4,20},{5,21},{6,22},{7,23},{8,24},{9,... | collective-permute-start | bytes 12296 | tf_op jit(solution)/shard_map/ppermute | solution.py:48
  224.4 5.1 %collective-permute-start.17 = (f32[8,128]{1,0:T(8,128)S(1)}, f32[8,128]{1,0:T(8,128)S(1)}, u32[]{:S(2)}, u32[]{:S(2)}) collective-permute-start(f32[8,128]{1,0:T(8,128)S(1)} %add.129), channel_id=1, source_target_pairs={{0,32},{1,33},{2,34},{3,35},{4,36},{5,37},{6,38},{7,39},{8,40},{9,... | collective-permute-start | bytes 12296 | tf_op jit(solution)/shard_map/ppermute | solution.py:48
where the time goes:
time: 235 us; the launch traced here: 232 us
  local copies, waits for them, and re-layouts  73.7 us (31%)
  starting transfers between devices  52.2 us (22%)
  waiting for transfers between devices  44.1 us (19%)
  matrix products  34.9 us (15%)
  other arithmetic  24.9 us (11%)
    ppermute x6, waiting for transfers between devices, halving_sum(): x = keep + lax.ppermute(send, axis, xor_pairs(count, bit))  23.5 us
    concatenate x8, local copies, waits for them, and re-layouts, body(): d_qkv = jnp.concatenate([d_query.astype(f32), key_sum, value_sum], axis=-1)  20.1 us
    ppermute x8, waiting for transfers between devices, doubling_sum(): x = x + lax.ppermute(x, axis, xor_pairs(count, bit))  18.5 us
    ppermute x2, starting transfers between devices, with_halo(): lax.ppermute(head, axis, [((i + 1) % count, i) for i in range(ends)])  12.5 us
    ppermute x6, starting transfers between devices, halving_sum(): x = keep + lax.ppermute(send, axis, xor_pairs(count, bit))  11.6 us
    ppermute x8, starting transfers between devices, doubling_sum(): x = x + lax.ppermute(x, axis, xor_pairs(count, bit))  10.7 us
    unnamed x51, local copies, waits for them, and re-layouts  9 us
    dot_general x1, matrix products, body(): jnp.einsum('ghab,bghd->aghd', score_grad, key_heads, preferred_element_ty...  8.25 us
  transfers between devices with their start and end apart: 21, of which 13 were waited for; matrix products, arithmetic and copies ran while one was open for 20% of the time, Pallas kernels for 0%

commit v1 on v0

--- a/solution.py
+++ b/solution.py
@@ -6,6 +6,12 @@
 
 HEADS = 8
 MAXOFF = 2
+
+
+def stacked_exchange(x, name, split, join):
+    pieces = jnp.split(x, lax.axis_size(name), axis=split)
+    received = lax.all_to_all(jnp.stack(pieces), name, 0, 0)
+    return jnp.concatenate(received, axis=join)
 
 
 def axis_bits(axis):
@@ -98,7 +104,7 @@
     flat_feats = warped.reshape(own_count, cell_count, channels)
     flat_grads = d_out.reshape(own_count, cell_count, channels)
     all_feats, all_grads = (
-        lax.all_to_all(flat_feats, "agent", split_axis=1, concat_axis=0, tiled=True),
+        stacked_exchange(flat_feats, "agent", 1, 0),
         lax.all_to_all(flat_grads, "agent", split_axis=1, concat_axis=0, tiled=True),
     )
     part_cells = all_feats.shape[1]

time: 235 us -> 236 us (level)
    unnamed x51 -> x53, local copies, waits for them, and re-layouts: 9 us -> 8.76 us
where the time goes in v1:
time: 236 us; the launch traced here: 233 us
  local copies, waits for them, and re-layouts  73.5 us (31%)
  starting transfers between devices  52.2 us (22%)
  waiting for transfers between devices  44.1 us (19%)
  matrix products  35 us (15%)
  other arithmetic  25.7 us (11%)
    ppermute x6, waiting for transfers between devices, halving_sum(): x = keep + lax.ppermute(send, axis, xor_pairs(count, bit))  23.4 us
    concatenate x8, local copies, waits for them, and re-layouts, body(): d_qkv = jnp.concatenate([d_query.astype(f32), key_sum, value_sum], axis=-1)  20.1 us
    ppermute x8, waiting for transfers between devices, doubling_sum(): x = x + lax.ppermute(x, axis, xor_pairs(count, bit))  18.5 us
    ppermute x2, starting transfers between devices, with_halo(): lax.ppermute(head, axis, [((i + 1) % count, i) for i in range(ends)])  12.5 us
    ppermute x6, starting transfers between devices, halving_sum(): x = keep + lax.ppermute(send, axis, xor_pairs(count, bit))  11.6 us
    ppermute x8, starting transfers between devices, doubling_sum(): x = x + lax.ppermute(x, axis, xor_pairs(count, bit))  10.7 us
    unnamed x53, local copies, waits for them, and re-layouts  8.76 us
    dot_general x1, matrix products, body(): jnp.einsum('ghab,bghd->aghd', score_grad, key_heads, preferred_element_ty...  8.23 us
  transfers between devices with their start and end apart: 21, of which 13 were waited for; matrix products, arithmetic and copies ran while one was open for 20% of the time, Pallas kernels for 0%

profile of v1, /device:TPU:2, one launch (start us, length us, event | category | flops | bytes accessed | tf_op | source)
XLA Modules:
  0.0 232.8 jit_solution(6998658115844097407)
XLA Ops:
  0.7 2.0 copy.81
  2.7 4.5 %all-to-all-start.1 = ((bf16[8,96,256]{2,0,1:T(8,128)(2,1)}), bf16[8,96,256]{2,0,1:T(8,128)(2,1)S(1)}, u32[]{:S(2)}, u32[]{:S(2)}) async-start(bf16[8,96,256]{2,0,1:T(8,128)(2,1)} %bitcast.11), calls=%async_computation.1 | async-start | bytes 786432 | tf_op jit(solution)/shard_map/all_to_all | solution.py:108
  7.2 1.2 copy.72
  8.4 1.9 collective-permute-start
  10.3 6.9 %collective-permute-start.1 = (bf16[8,2,24,256]{3,0,2,1:T(8,128)(2,1)S(1)}, bf16[8,2,24,256]{3,0,2,1:T(8,128)(2,1)S(1)}, u32[]{:S(2)}, u32[]{:S(2)}) collective-permute-start(bf16[8,2,24,256]{3,0,2,1:T(8,128)(2,1)S(1)} %get-tuple-element.34), channel_id=1, source_target_pairs={{1,0},{2,1},{3,2},{4,3},{5,4},{6,5},{7,6},{8,7},{9,8},{10,9},{11,1... | collective-permute-start | bytes 589832 | tf_op jit(solution)/shard_map/ppermute | solution.py:68
  18.7 1.8 collective-permute-done.1
  20.5 1.7 gather_fusion
  23.1 5.0 %all-to-all-start = ((bf16[4,8,24,256]{3,2,1,0:T(8,128)(2,1)}), bf16[4,8,24,256]{3,2,1,0:T(8,128)(2,1)S(1)}, u32[]{:S(2)}, u32[]{:S(2)}) async-start(bf16[4,8,24,256]{3,2,1,0:T(8,128)(2,1)} %pad_maximum_fusion.2), calls=%async_computation | async-start | bytes 786432 | tf_op jit(solution)/shard_map/all_to_all | solution.py:13
  30.3 1.8 squeeze.33
  32.3 1.8 squeeze.36
  34.1 1.8 squeeze.34
  35.9 3.4 %broadcast_select_fusion = bf16[32,24,8,32]{3,2,1,0:T(8,128)(2,1)} fusion(bf16[32,24,8,32]{3,2,1,0:T(8,128)(2,1)} %squeeze.33, bf16[32,24,8,32]{3,2,1,0:T(8,128)(2,1)} %squeeze.34, pred[32]{0:T(512)(128)(4,1)S(1)} %get-tuple-element.39), kind=kLoop, calls=%fused_computation.44 | loop fusion | flops 196608 | bytes 1179680 | tf_op jit(solution)/shard_map/jit(_where)/select_n | solution.py:144
  39.3 1.5 broadcast_select_fusion.1
  42.0 1.8 reshape_reshape.8
  43.8 1.8 reshape.315
  45.6 1.6 copy.131
  48.2 3.8 %fusion.3 = (f32[24,8,32]{2,1,0:T(8,128)S(1)}, f32[24,8,32,32]{2,3,1,0:T(8,128)S(1)}) fusion(pred[32,32]{0,1:T(8,128)(4,1)S(1)} %fusion.44, bf16[32,24,8,32]{0,3,2,1:T(8,128)(2,1)S(1)} %bitcast.138, bf16[32,24,8,32]{3,2,1,0:T(8,128)(2,1)} %reshape.315), kind=kOutput, calls=%fused_computation.12 | convolution fusion | flops 13166592 | bytes 1598464 | tf_op jit(solution)/shard_map/aghd,bghd->ghab/dot_general | solution.py:126
  52.0 1.6 copy-done.5
  54.5 1.8 copy.97
  56.2 3.3 %fusion.26 = bf16[32,24,8,32]{0,3,2,1:T(8,128)(2,1)} fusion(bf16[32,24,8,32]{0,3,2,1:T(8,128)(2,1)} %bitcast.119, bf16[24,8,32,32]{2,3,1,0:T(8,128)(2,1)S(1)} %fusion.59), kind=kOutput, calls=%fused_computation.46 | convolution fusion | flops 12779520 | bytes 1179648 | tf_op jit(solution)/shard_map/ghab,bghd->aghd/dot_general | solution.py:135
  59.6 2.9 %fusion.22 = f32[24,8,32,32]{2,3,1,0:T(8,128)} fusion(bf16[32,24,8,32]{0,3,2,1:T(8,128)(2,1)S(1)} %bitcast.120, bf16[32,24,8,32]{3,2,1,0:T(8,128)(2,1)S(1)} %copy-done.3), kind=kOutput, calls=%fused_computation.40 | convolution fusion | flops 12582912 | bytes 1572864 | tf_op jit(solution)/shard_map/aghd,bghd->ghab/dot_general | solution.py:153
  62.5 8.2 %fusion.15 = f32[24,8,32,32]{3,2,1,0:T(8,128)} fusion(bf16[32,24,8,32]{0,3,2,1:T(8,128)(2,1)S(1)} %bitcast.139, f32[24,8,32,32]{2,3,1,0:T(8,128)} %fusion.22, f32[24,8,32,32]{2,3,1,0:T(8,128)} %copy-done.5, f32[24,8,32]{2,1,0:T(8,128)S(1)} %get-tuple-element.40, pred[32,32]{0,1:T(8,128)(4,1)S(1)} %fusion.44), kind=kOutput, calls=%fused_computation.31 | convolution fusion | flops 15144991 | bytes 2778112 | tf_op jit(solution)/shard_map/ghab,bghd->aghd/dot_general | solution.py:162
  70.7 6.7 %multiply_convert_fusion = bf16[24,8,32,32]{2,3,1,0:T(8,128)(2,1)S(1)} fusion(f32[24,8,32,32]{2,3,1,0:T(8,128)} %fusion.22, f32[24,8,32]{2,1,0:T(8,128)} %copy-done.17, f32[24,8,32,32]{2,3,1,0:T(8,128)} %copy-done.5, pred[32,32]{0,1:T(8,128)(4,1)S(1)} %fusion.44), kind=kOutput, calls=%fused_computation.5 | output fusion | flops 2168863 | bytes 1991680 | tf_op jit(solution)/shard_map/sub | solution.py:158
  77.4 4.5 %convert_reduce_fusion = f32[24,8,32,32]{3,2,1,0:T(8,128)} fusion(bf16[4,8,24,8,32]{4,3,2,1,0:T(8,128)(2,1)S(1)} %copy-done.7, bf16[24,8,32,32]{3,2,1,0:T(8,128)(2,1)S(1)} %copy-done.8), kind=kOutput, calls=%fused_computation.3 | convolution fusion | flops 14745600 | bytes 1572864 | tf_op jit(solution)/shard_map/ghnyb,nyghd->nbghd/dot_general | solution.py:174
  82.0 2.3 copy.122
  84.3 1.6 copy.91
  85.8 2.3 copy.104
  88.2 6.2 %convert_reduce_fusion.1 = f32[24,8,32,32]{3,2,1,0:T(8,128)} fusion(bf16[4,8,24,8,32]{4,3,2,1,0:T(8,128)(2,1)} %reshape_reshape.8, bf16[24,8,32,32]{3,2,1,0:T(8,128)(2,1)} %copy.91), kind=kOutput, calls=%fused_computation.4 | convolution fusion | flops 14745600 | bytes 1572864 | tf_op jit(solution)/shard_map/ghnyb,nyghd->nbghd/dot_general | solution.py:171
  94.3 2.3 copy.121
  96.6 1.2 subtract_convert_fusion
  99.9 3.8 %copy.108 = bf16[32,24,8,32]{3,2,1,0:T(8,128)(2,1)S(1)} copy(bf16[32,24,8,32]{0,3,2,1:T(8,128)(2,1)} %fusion.26) | data formatting | bytes 786432 | tf_op jit(solution)/shard_map/convert_element_type | solution.py:136
  103.7 1.8 broadcast_in_dim.105
  105.5 2.8 %fusion.12 = f32[2,2,256,768]{2,3,1,0:T(8,128)S(1)} fusion(bf16[1,32,24,768]{3,1,2,0:T(8,128)(2,1)S(1)} %copy-done.14, bf16[1,32,24,768]{3,1,2,0:T(8,128)(2,1)} %fusion.16, pred[2,32]{1,0:T(4,128)(4,1)S(1)} %copy-done.21, bf16[32,24,256]{2,0,1:T(8,128)(2,1)} %copy.105), kind=kOutput, calls=%fused_computation.26 | convolution fusion | flops 1213071360 | bytes 5898304 | tf_op jit(solution)/shard_map/tpc,spe->stce/dot_general | solution.py:191
  110.3 2.4 %copy.110 = f32[2,256,1024]{2,0,1:T(2,128)} copy(f32[2,256,1024]{1,2,0:T(8,128)S(1)} %pad_maximum_fusion.1) | data formatting | bytes 4194304 | tf_op jit(solution)/shard_map/concatenate | solution.py:196
  112.7 2.4 %fusion.62 = (f32[2,2,2,2,2,1,2,4,1024]{8,6,7,5,4,3,2,1,0:T(2,128)S(1)}, f32[2,2,2,2,2,1,2,4,1024]{8,6,7,5,4,3,2,1,0:T(2,128)S(1)}) fusion(f32[2,2,2,2,2,2,2,4,1024]{8,6,7,5,4,3,2,1,0:T(2,128)} %bitcast.127), kind=kLoop, calls=%fused_computation.119 | loop fusion | bytes 4194304 | tf_op jit(solution)/shard_map/slice | solution.py:44
  117.0 2.8 %collective-permute-done.4 = f32[2,2,2,2,2,1,2,4,1024]{8,7,6,5,4,3,2,1,0:T(4,128)} collective-permute-done((f32[2,2,2,2,2,1,2,4,1024]{8,7,6,5,4,3,2,1,0:T(4,128)S(1)}, f32[2,2,2,2,2,1,2,4,1024]{8,7,6,5,4,3,2,1,0:T(4,128)}, u32[]{:S(2)}, u32[]{:S(2)}) %collective-permute-start.4) | collective-permute-done | bytes 1048608 | tf_op jit(solution)/shard_map/ppermute | solution.py:47
  119.8 2.6 %select_add_fusion = f32[2,2,2,2,2,1,2,4,1024]{8,7,6,5,4,3,2,1,0:T(4,128)S(1)} fusion(f32[2,2,2,2,2,1,2,4,1024]{8,7,6,5,4,3,2,1,0:T(4,128)} %collective-permute-done.4, f32[2,2,2,2,2,1,2,4,1024]{8,6,7,5,4,3,2,1,0:T(2,128)} %copy-done.2, f32[2,2,2,2,2,1,2,4,1024]{8,6,7,5,4,3,2,1,0:T(2,128)S(1)} %get-tuple-element.18, pred[]{:T(512)S(6)} %eq.62), kind=kLoop, calls=%fused_computation.50 | loop fusion | flops 524288 | bytes 4194305 | tf_op jit(solution)/shard_map/add | solution.py:47
  123.9 5.1 %copy.90 = f32[32,24,8,32]{3,2,1,0:T(8,128)} copy(f32[32,24,8,32]{0,3,2,1:T(8,128)} %bitcast.124) | data formatting | bytes 1572864 | tf_op jit(solution)/shard_map/concatenate | solution.py:179
  129.0 2.4 %reshape.324 = f32[1,768,256]{2,1,0:T(8,128)S(1)} reshape(f32[32,24,8,32]{3,2,1,0:T(8,128)} %copy.90) | data formatting | bytes 1572864 | tf_op jit(solution)/shard_map/concatenate | solution.py:179
  131.4 4.8 %copy.94 = f32[32,24,8,32]{3,2,1,0:T(8,128)} copy(f32[32,24,8,32]{0,3,2,1:T(8,128)} %bitcast.126) | data formatting | bytes 1572864 | tf_op jit(solution)/shard_map/reduce_sum | solution.py:177
  136.2 2.4 %concatenate.75 = f32[1,768,256]{2,1,0:T(8,128)S(1)} reshape(f32[32,24,8,32]{3,2,1,0:T(8,128)} %copy.94) | data formatting | bytes 1572864 | tf_op jit(solution)/shard_map/concatenate | solution.py:179
  138.6 4.8 %copy.100 = f32[32,24,8,32]{3,2,1,0:T(8,128)} copy(f32[32,24,8,32]{0,3,2,1:T(8,128)} %bitcast.122) | data formatting | bytes 1572864 | tf_op jit(solution)/shard_map/reduce_sum | solution.py:178
  143.4 3.1 %concatenate.76 = f32[1,768,256]{2,1,0:T(8,128)} reshape(f32[32,24,8,32]{3,2,1,0:T(8,128)} %copy.100) | data formatting | bytes 1572864 | tf_op jit(solution)/shard_map/concatenate | solution.py:179
  147.7 1.3 select_add_fusion.1
  150.0 7.5 %collective-permute-done.6 = f32[2,1,2,2,1,1,2,4,1024]{8,7,6,5,4,3,2,1,0:T(4,128)S(1)} collective-permute-done((f32[2,1,2,2,1,1,2,4,1024]{8,7,6,5,4,3,2,1,0:T(4,128)S(1)}, f32[2,1,2,2,1,1,2,4,1024]{8,7,6,5,4,3,2,1,0:T(4,128)S(1)}, u32[]{:S(2)}, u32[]{:S(2)}) %collective-permute-start.6) | collective-permute-done | bytes 262176 | tf_op jit(solution)/shard_map/ppermute | solution.py:47
  157.7 5.8 %collective-permute-start.7 = (f32[2,1,2,1,1,1,2,4,1024]{8,7,6,5,4,3,2,1,0:T(4,128)S(1)}, f32[2,1,2,1,1,1,2,4,1024]{8,7,6,5,4,3,2,1,0:T(4,128)S(1)}, u32[]{:S(2)}, u32[]{:S(2)}) collective-permute-start(f32[2,1,2,1,1,1,2,4,1024]{8,7,6,5,4,3,2,1,0:T(4,128)S(1)} %slice_select_fusion.2), channel_id=1, source_target_pairs={{0,4},{1,5},{2,6},{3,7},{4,0},{5,1},{6,2},{7,3},{8,12},{9,13},{10,... | collective-permute-start | bytes 393224 | tf_op jit(solution)/shard_map/ppermute | solution.py:47
  163.4 1.4 fusion.13
  164.9 4.3 %collective-permute-done.7 = f32[2,1,2,1,1,1,2,4,1024]{8,7,6,5,4,3,2,1,0:T(4,128)S(1)} collective-permute-done((f32[2,1,2,1,1,1,2,4,1024]{8,7,6,5,4,3,2,1,0:T(4,128)S(1)}, f32[2,1,2,1,1,1,2,4,1024]{8,7,6,5,4,3,2,1,0:T(4,128)S(1)}, u32[]{:S(2)}, u32[]{:S(2)}) %collective-permute-start.7) | collective-permute-done | bytes 131104 | tf_op jit(solution)/shard_map/ppermute | solution.py:47
  169.2 2.2 collective-permute-start.8
  171.6 3.5 %collective-permute-done.8 = f32[1,1,2,1,1,1,2,4,1024]{8,7,6,5,4,3,2,1,0:T(4,128)S(1)} collective-permute-done((f32[1,1,2,1,1,1,2,4,1024]{8,7,6,5,4,3,2,1,0:T(4,128)S(1)}, f32[1,1,2,1,1,1,2,4,1024]{8,7,6,5,4,3,2,1,0:T(4,128)S(1)}, u32[]{:S(2)}, u32[]{:S(2)}) %collective-permute-start.8) | collective-permute-done | bytes 65568 | tf_op jit(solution)/shard_map/ppermute | solution.py:47
  175.1 2.4 %collective-permute-start.9 = (f32[1,1,1,1,1,1,2,4,1024]{8,7,6,5,4,3,2,1,0:T(4,128)S(1)}, f32[1,1,1,1,1,1,2,4,1024]{8,7,6,5,4,3,2,1,0:T(4,128)S(1)}, u32[]{:S(2)}, u32[]{:S(2)}) collective-permute-start(f32[1,1,1,1,1,1,2,4,1024]{8,7,6,5,4,3,2,1,0:T(4,128)S(1)} %slice_select_fusion.4), channel_id=1, source_target_pairs={{0,8},{1,9},{2,10},{3,11},{4,12},{5,13},{6,14},{7,15},{8,0},{9,1},... | collective-permute-start | bytes 98312 | tf_op jit(solution)/shard_map/ppermute | solution.py:47
  177.6 5.4 %collective-permute-done.9 = f32[1,1,1,1,1,1,2,4,1024]{8,7,6,5,4,3,2,1,0:T(4,128)S(1)} collective-permute-done((f32[1,1,1,1,1,1,2,4,1024]{8,7,6,5,4,3,2,1,0:T(4,128)S(1)}, f32[1,1,1,1,1,1,2,4,1024]{8,7,6,5,4,3,2,1,0:T(4,128)S(1)}, u32[]{:S(2)}, u32[]{:S(2)}) %collective-permute-start.9) | collective-permute-done | bytes 32800 | tf_op jit(solution)/shard_map/ppermute | solution.py:47
  183.1 1.8 collective-permute-start.10
  185.8 3.9 %all-to-all-start.2 = ((bf16[32,24,256]{2,1,0:T(8,128)(2,1)}), bf16[32,24,256]{2,1,0:T(8,128)(2,1)S(1)}, u32[]{:S(2)}, u32[]{:S(2)}) async-start(bf16[32,24,256]{2,1,0:T(8,128)(2,1)} %select_convert_fusion), calls=%async_computation.2 | async-start | bytes 786432 | tf_op jit(solution)/shard_map/all_to_all | solution.py:186
  189.7 3.6 %collective-permute-start.11 = (f32[2,4,1024]{2,1,0:T(4,128)S(1)}, f32[2,4,1024]{2,1,0:T(4,128)S(1)}, u32[]{:S(2)}, u32[]{:S(2)}) collective-permute-start(f32[2,4,1024]{2,1,0:T(4,128)S(1)} %add.123), channel_id=1, source_target_pairs={{0,128},{64,192},{128,0},{192,64},{1,129},{65,193},{129,1},{193,65... | collective-permute-start | bytes 98312 | tf_op jit(solution)/shard_map/ppermute | solution.py:54
  193.3 4.1 %collective-permute-done.11 = f32[2,4,1024]{2,1,0:T(4,128)S(1)} collective-permute-done((f32[2,4,1024]{2,1,0:T(4,128)S(1)}, f32[2,4,1024]{2,1,0:T(4,128)S(1)}, u32[]{:S(2)}, u32[]{:S(2)}) %collective-permute-start.11) | collective-permute-done | bytes 32800 | tf_op jit(solution)/shard_map/ppermute | solution.py:54
  200.9 2.1 collective-permute-start.2
  203.0 5.6 %collective-permute-start.3 = (bf16[8,2,24,256]{3,0,2,1:T(8,128)(2,1)S(1)}, bf16[8,2,24,256]{3,0,2,1:T(8,128)(2,1)S(1)}, u32[]{:S(2)}, u32[]{:S(2)}) collective-permute-start(bf16[8,2,24,256]{3,0,2,1:T(8,128)(2,1)S(1)} %get-tuple-element.28), channel_id=1, source_target_pairs={{1,0},{2,1},{3,2},{4,3},{5,4},{6,5},{7,6},{8,7},{9,8},{10,9},{11,1... | collective-permute-start | bytes 589832 | tf_op jit(solution)/shard_map/ppermute | solution.py:68
  210.5 3.4 %collective-permute-done.14 = f32[8,128]{1,0:T(8,128)S(1)} collective-permute-done((f32[8,128]{1,0:T(8,128)S(1)}, f32[8,128]{1,0:T(8,128)S(1)}, u32[]{:S(2)}, u32[]{:S(2)}) %collective-permute-start.14) | collective-permute-done | bytes 4128 | tf_op jit(solution)/shard_map/ppermute | solution.py:54
  213.9 1.4 collective-permute-start.15
  215.3 6.1 %collective-permute-done.15 = f32[8,128]{1,0:T(8,128)S(1)} collective-permute-done((f32[8,128]{1,0:T(8,128)S(1)}, f32[8,128]{1,0:T(8,128)S(1)}, u32[]{:S(2)}, u32[]{:S(2)}) %collective-permute-start.15) | collective-permute-done | bytes 4128 | tf_op jit(solution)/shard_map/ppermute | solution.py:54
  221.5 3.5 %collective-permute-done.16 = f32[8,128]{1,0:T(8,128)S(1)} collective-permute-done((f32[8,128]{1,0:T(8,128)S(1)}, f32[8,128]{1,0:T(8,128)S(1)}, u32[]{:S(2)}, u32[]{:S(2)}) %collective-permute-start.16) | collective-permute-done | bytes 4128 | tf_op jit(solution)/shard_map/ppermute | solution.py:54
  225.0 2.1 collective-permute-start.17
  227.2 1.7 gather_fusion.1
  (131 shorter events, 26.8 us)
Async XLA Ops:
  0.6 40.2 %copy-start = (bf16[2,256,768]{2,1,0:T(8,128)(2,1)S(1)}, bf16[2,256,768]{2,1,0:T(8,128)(2,1)}, u32[]{:S(2)}) copy-start(bf16[2,256,768]{2,1,0:T(8,128)(2,1)} %param.11) | copy-start | bytes 2359300
  0.6 16.6 %copy-start.23 = (s32[32]{0:T(128)S(1)}, s32[32]{0:T(128)}, u32[]{:S(2)}) copy-start(s32[32]{0:T(128)} %param.9) | copy-start | bytes 388
  0.7 16.6 %copy-start.22 = (s32[32]{0:T(128)S(1)}, s32[32]{0:T(128)}, u32[]{:S(2)}) copy-start(s32[32]{0:T(128)} %param.8) | copy-start | bytes 388
  0.7 17.5 %copy-start.18 = (s32[32,2]{0,1:T(2,128)S(1)}, s32[32,2]{0,1:T(2,128)}, u32[]{:S(2)}) copy-start(s32[32,2]{0,1:T(2,128)} %param.10) | copy-start | bytes 772
  2.7 20.4 %all-to-all-start.1 = ((bf16[8,96,256]{2,0,1:T(8,128)(2,1)}), bf16[8,96,256]{2,0,1:T(8,128)(2,1)S(1)}, u32[]{:S(2)}, u32[]{:S(2)}) async-start(bf16[8,96,256]{2,0,1:T(8,128)(2,1)} %bitcast.11), calls=%async_computation.1 | async-start | bytes 786432 | tf_op jit(solution)/shard_map/all_to_all | solution.py:108
  8.4 10.2 %collective-permute-start = (bf16[8,2,24,256]{3,0,2,1:T(8,128)(2,1)S(1)}, bf16[8,2,24,256]{3,0,2,1:T(8,128)(2,1)S(1)}, u32[]{:S(2)}, u32[]{:S(2)}) collective-permute-start(bf16[8,2,24,256]{3,0,2,1:T(8,128)(2,1)S(1)} %get-tuple-element.33), channel_id=1, source_target_pairs={{0,1},{1,2},{2,3},{3,4},{4,5},{5,6},{6,7},{7,8},{8,9},{9,10},{10,1... | collective-permute-start | bytes 589832 | tf_op jit(solution)/shard_map/ppermute | solution.py:66
  10.3 10.1 %collective-permute-start.1 = (bf16[8,2,24,256]{3,0,2,1:T(8,128)(2,1)S(1)}, bf16[8,2,24,256]{3,0,2,1:T(8,128)(2,1)S(1)}, u32[]{:S(2)}, u32[]{:S(2)}) collective-permute-start(bf16[8,2,24,256]{3,0,2,1:T(8,128)(2,1)S(1)} %get-tuple-element.34), channel_id=1, source_target_pairs={{1,0},{2,1},{3,2},{4,3},{5,4},{6,5},{7,6},{8,7},{9,8},{10,9},{11,1... | collective-permute-start | bytes 589832 | tf_op jit(solution)/shard_map/ppermute | solution.py:68
  18.0 0.7 copy-start.20
  22.2 6.1 %copy-start.16 = (bf16[2,256,256]{2,1,0:T(8,128)(2,1)S(1)}, bf16[2,256,256]{2,1,0:T(8,128)(2,1)}, u32[]{:S(2)}) copy-start(bf16[2,256,256]{2,1,0:T(8,128)(2,1)} %param.12) | copy-start | bytes 786436
  23.1 17.6 %all-to-all-start = ((bf16[4,8,24,256]{3,2,1,0:T(8,128)(2,1)}), bf16[4,8,24,256]{3,2,1,0:T(8,128)(2,1)S(1)}, u32[]{:S(2)}, u32[]{:S(2)}) async-start(bf16[4,8,24,256]{3,2,1,0:T(8,128)(2,1)} %pad_maximum_fusion.2), calls=%async_computation | async-start | bytes 786432 | tf_op jit(solution)/shard_map/all_to_all | solution.py:13
  28.3 1.2 copy-start.9
  29.7 2.5 %copy-start.11 = (bf16[1,768,256]{1,2,0:T(8,128)(2,1)S(1)}, bf16[1,768,256]{1,2,0:T(8,128)(2,1)}, u32[]{:S(2)}) copy-start(bf16[1,768,256]{1,2,0:T(8,128)(2,1)} %get-tuple-element.25) | copy-start | bytes 1179652
  35.9 3.4 %copy-start.4 = (bf16[4,8,24,8,32]{4,3,2,1,0:T(8,128)(2,1)S(1)}, bf16[4,8,24,8,32]{4,3,2,1,0:T(8,128)(2,1)}, u32[]{:S(2)}) copy-start(bf16[4,8,24,8,32]{4,3,2,1,0:T(8,128)(2,1)} %squeeze.36) | copy-start | bytes 1179652
  35.9 3.4 %copy-start.19 = (pred[4,8]{1,0:T(4,128)(4,1)S(1)}, pred[4,8]{1,0:T(4,128)(4,1)}, u32[]{:S(2)}) copy-start(pred[4,8]{1,0:T(4,128)(4,1)} %broadcast_in_dim.96) | copy-start | bytes 100
  48.1 3.8 %copy-start.12 = (bf16[32,24,256]{0,2,1:T(8,128)(2,1)}, bf16[32,24,256]{0,2,1:T(8,128)(2,1)S(1)}, u32[]{:S(2)}) copy-start(bf16[32,24,256]{0,2,1:T(8,128)(2,1)S(1)} %copy.130) | copy-start | bytes 1179652
  52.0 1.7 copy-start.5
  52.0 10.5 %copy-start.17 = (f32[24,8,32]{2,1,0:T(8,128)}, f32[24,8,32]{2,1,0:T(8,128)S(1)}, u32[]{:S(2)}) copy-start(f32[24,8,32]{2,1,0:T(8,128)S(1)} %get-tuple-element.40) | copy-start | bytes 73732
  56.2 3.4 %copy-start.1 = (bf16[32,24,256]{0,2,1:T(8,128)(2,1)S(1)}, bf16[32,24,256]{0,2,1:T(8,128)(2,1)}, u32[]{:S(2)}) copy-start(bf16[32,24,256]{0,2,1:T(8,128)(2,1)} %copy.131) | copy-start | bytes 1179652
  56.2 3.4 %copy-start.3 = (bf16[32,24,8,32]{3,2,1,0:T(8,128)(2,1)S(1)}, bf16[32,24,8,32]{3,2,1,0:T(8,128)(2,1)}, u32[]{:S(2)}) copy-start(bf16[32,24,8,32]{3,2,1,0:T(8,128)(2,1)} %broadcast_select_fusion) | copy-start | bytes 1179652
  59.6 2.9 %copy-start.13 = (bf16[32,24,256]{0,2,1:T(8,128)(2,1)S(1)}, bf16[32,24,256]{0,2,1:T(8,128)(2,1)}, u32[]{:S(2)}) copy-start(bf16[32,24,256]{0,2,1:T(8,128)(2,1)} %copy-done.12) | copy-start | bytes 1179652
  70.7 6.7 %copy-start.7 = (bf16[4,8,24,8,32]{4,3,2,1,0:T(8,128)(2,1)S(1)}, bf16[4,8,24,8,32]{4,3,2,1,0:T(8,128)(2,1)}, u32[]{:S(2)}) copy-start(bf16[4,8,24,8,32]{4,3,2,1,0:T(8,128)(2,1)} %broadcast_select_fusion.1) | copy-start | bytes 1179652
  70.7 6.7 %copy-start.8 = (bf16[24,8,32,32]{3,2,1,0:T(8,128)(2,1)S(1)}, bf16[24,8,32,32]{3,2,1,0:T(8,128)(2,1)}, u32[]{:S(2)}) copy-start(bf16[24,8,32,32]{3,2,1,0:T(8,128)(2,1)} %copy.97) | copy-start | bytes 1179652
  99.9 5.7 %copy-start.14 = (bf16[1,32,24,768]{3,1,2,0:T(8,128)(2,1)S(1)}, bf16[1,32,24,768]{3,1,2,0:T(8,128)(2,1)}, u32[]{:S(2)}) copy-start(bf16[1,32,24,768]{3,1,2,0:T(8,128)(2,1)} %subtract_convert_fusion) | copy-start | bytes 3538948
  99.9 5.7 %copy-start.21 = (pred[2,32]{1,0:T(4,128)(4,1)S(1)}, pred[2,32]{1,0:T(4,128)(4,1)}, u32[]{:S(2)}) copy-start(pred[2,32]{1,0:T(4,128)(4,1)} %copy-done.20) | copy-start | bytes 196
  108.4 1.0 copy-start.10
  108.4 1.1 copy-start.15
  115.1 1.0 copy-start.2
  116.9 2.9 %collective-permute-start.4 = (f32[2,2,2,2,2,1,2,4,1024]{8,7,6,5,4,3,2,1,0:T(4,128)S(1)}, f32[2,2,2,2,2,1,2,4,1024]{8,7,6,5,4,3,2,1,0:T(4,128)}, u32[]{:S(2)}, u32[]{:S(2)}) collective-permute-start(f32[2,2,2,2,2,1,2,4,1024]{8,7,6,5,4,3,2,1,0:T(4,128)S(1)} %copy_select_fusion), channel_id=1, source_target_pairs={{0,1},{1,0},{2,3},{3,2},{4,5},{5,4},{6,7},{7,6},{8,9},{9,8},{10,11... | collective-permute-start | bytes 3145736 | tf_op jit(solution)/shard_map/ppermute | solution.py:47
  123.4 24.4 %collective-permute-start.5 = (f32[2,2,2,2,1,1,2,4,1024]{8,7,6,5,4,3,2,1,0:T(4,128)}, f32[2,2,2,2,1,1,2,4,1024]{8,7,6,5,4,3,2,1,0:T(4,128)}, u32[]{:S(2)}, u32[]{:S(2)}) collective-permute-start(f32[2,2,2,2,1,1,2,4,1024]{8,7,6,5,4,3,2,1,0:T(4,128)} %slice_select_fusion), channel_id=1, source_target_pairs={{0,2},{1,3},{2,0},{3,1},{4,6},{5,7},{6,4},{7,5},{8,10},{9,11},{10,... | collective-permute-start | bytes 1572872 | tf_op jit(solution)/shard_map/ppermute | solution.py:47
  146.5 1.1 copy-start.6
  149.1 8.4 %collective-permute-start.6 = (f32[2,1,2,2,1,1,2,4,1024]{8,7,6,5,4,3,2,1,0:T(4,128)S(1)}, f32[2,1,2,2,1,1,2,4,1024]{8,7,6,5,4,3,2,1,0:T(4,128)S(1)}, u32[]{:S(2)}, u32[]{:S(2)}) collective-permute-start(f32[2,1,2,2,1,1,2,4,1024]{8,7,6,5,4,3,2,1,0:T(4,128)S(1)} %slice_select_fusion.1), channel_id=1, source_target_pairs={{0,16},{1,17},{2,18},{3,19},{4,20},{5,21},{6,22},{7,23},{8,24},{9,... | collective-permute-start | bytes 786440 | tf_op jit(solution)/shard_map/ppermute | solution.py:47
  157.7 11.5 %collective-permute-start.7 = (f32[2,1,2,1,1,1,2,4,1024]{8,7,6,5,4,3,2,1,0:T(4,128)S(1)}, f32[2,1,2,1,1,1,2,4,1024]{8,7,6,5,4,3,2,1,0:T(4,128)S(1)}, u32[]{:S(2)}, u32[]{:S(2)}) collective-permute-start(f32[2,1,2,1,1,1,2,4,1024]{8,7,6,5,4,3,2,1,0:T(4,128)S(1)} %slice_select_fusion.2), channel_id=1, source_target_pairs={{0,4},{1,5},{2,6},{3,7},{4,0},{5,1},{6,2},{7,3},{8,12},{9,13},{10,... | collective-permute-start | bytes 393224 | tf_op jit(solution)/shard_map/ppermute | solution.py:47
  169.2 5.9 %collective-permute-start.8 = (f32[1,1,2,1,1,1,2,4,1024]{8,7,6,5,4,3,2,1,0:T(4,128)S(1)}, f32[1,1,2,1,1,1,2,4,1024]{8,7,6,5,4,3,2,1,0:T(4,128)S(1)}, u32[]{:S(2)}, u32[]{:S(2)}) collective-permute-start(f32[1,1,2,1,1,1,2,4,1024]{8,7,6,5,4,3,2,1,0:T(4,128)S(1)} %slice_select_fusion.3), channel_id=1, source_target_pairs={{0,32},{1,33},{2,34},{3,35},{4,36},{5,37},{6,38},{7,39},{8,40},{9,... | collective-permute-start | bytes 196616 | tf_op jit(solution)/shard_map/ppermute | solution.py:47
  175.1 7.9 %collective-permute-start.9 = (f32[1,1,1,1,1,1,2,4,1024]{8,7,6,5,4,3,2,1,0:T(4,128)S(1)}, f32[1,1,1,1,1,1,2,4,1024]{8,7,6,5,4,3,2,1,0:T(4,128)S(1)}, u32[]{:S(2)}, u32[]{:S(2)}) collective-permute-start(f32[1,1,1,1,1,1,2,4,1024]{8,7,6,5,4,3,2,1,0:T(4,128)S(1)} %slice_select_fusion.4), channel_id=1, source_target_pairs={{0,8},{1,9},{2,10},{3,11},{4,12},{5,13},{6,14},{7,15},{8,0},{9,1},... | collective-permute-start | bytes 98312 | tf_op jit(solution)/shard_map/ppermute | solution.py:47
  183.1 6.6 %collective-permute-start.10 = (f32[2,4,1024]{2,1,0:T(4,128)S(1)}, f32[2,4,1024]{2,1,0:T(4,128)S(1)}, u32[]{:S(2)}, u32[]{:S(2)}) collective-permute-start(f32[2,4,1024]{2,1,0:T(4,128)S(1)} %add_bitcast_fusion), channel_id=1, source_target_pairs={{0,64},{64,0},{128,192},{192,128},{1,65},{65,1},{129,193},{193,129... | collective-permute-start | bytes 98312 | tf_op jit(solution)/shard_map/ppermute | solution.py:54
  185.8 13.2 %all-to-all-start.2 = ((bf16[32,24,256]{2,1,0:T(8,128)(2,1)}), bf16[32,24,256]{2,1,0:T(8,128)(2,1)S(1)}, u32[]{:S(2)}, u32[]{:S(2)}) async-start(bf16[32,24,256]{2,1,0:T(8,128)(2,1)} %select_convert_fusion), calls=%async_computation.2 | async-start | bytes 786432 | tf_op jit(solution)/shard_map/all_to_all | solution.py:186
  189.7 7.7 %collective-permute-start.11 = (f32[2,4,1024]{2,1,0:T(4,128)S(1)}, f32[2,4,1024]{2,1,0:T(4,128)S(1)}, u32[]{:S(2)}, u32[]{:S(2)}) collective-permute-start(f32[2,4,1024]{2,1,0:T(4,128)S(1)} %add.123), channel_id=1, source_target_pairs={{0,128},{64,192},{128,0},{192,64},{1,129},{65,193},{129,1},{193,65... | collective-permute-start | bytes 98312 | tf_op jit(solution)/shard_map/ppermute | solution.py:54
  198.7 1.4 collective-permute-start.12
  200.8 7.8 %collective-permute-start.13 = (f32[8,128]{1,0:T(8,128)S(1)}, f32[8,128]{1,0:T(8,128)S(1)}, u32[]{:S(2)}, u32[]{:S(2)}) collective-permute-start(f32[8,128]{1,0:T(8,128)S(1)} %broadcast_add_fusion), channel_id=1, source_target_pairs={{0,2},{1,3},{2,0},{3,1},{4,6},{5,7},{6,4},{7,5},{8,10},{9,11},{10,... | collective-permute-start | bytes 12296 | tf_op jit(solution)/shard_map/ppermute | solution.py:54
  200.9 26.2 %collective-permute-start.2 = (bf16[8,2,24,256]{3,0,2,1:T(8,128)(2,1)S(1)}, bf16[8,2,24,256]{3,0,2,1:T(8,128)(2,1)S(1)}, u32[]{:S(2)}, u32[]{:S(2)}) collective-permute-start(bf16[8,2,24,256]{3,0,2,1:T(8,128)(2,1)S(1)} %get-tuple-element.27), channel_id=1, source_target_pairs={{0,1},{1,2},{2,3},{3,4},{4,5},{5,6},{6,7},{7,8},{8,9},{9,10},{10,1... | collective-permute-start | bytes 589832 | tf_op jit(solution)/shard_map/ppermute | solution.py:66
  203.0 24.1 %collective-permute-start.3 = (bf16[8,2,24,256]{3,0,2,1:T(8,128)(2,1)S(1)}, bf16[8,2,24,256]{3,0,2,1:T(8,128)(2,1)S(1)}, u32[]{:S(2)}, u32[]{:S(2)}) collective-permute-start(bf16[8,2,24,256]{3,0,2,1:T(8,128)(2,1)S(1)} %get-tuple-element.28), channel_id=1, source_target_pairs={{1,0},{2,1},{3,2},{4,3},{5,4},{6,5},{7,6},{8,7},{9,8},{10,9},{11,1... | collective-permute-start | bytes 589832 | tf_op jit(solution)/shard_map/ppermute | solution.py:68
  209.3 4.6 %collective-permute-start.14 = (f32[8,128]{1,0:T(8,128)S(1)}, f32[8,128]{1,0:T(8,128)S(1)}, u32[]{:S(2)}, u32[]{:S(2)}) collective-permute-start(f32[8,128]{1,0:T(8,128)S(1)} %fusion.79), channel_id=1, source_target_pairs={{0,4},{1,5},{2,6},{3,7},{4,0},{5,1},{6,2},{7,3},{8,12},{9,13},{10,... | collective-permute-start | bytes 12296 | tf_op jit(solution)/shard_map/ppermute | solution.py:54
  213.9 7.5 %collective-permute-start.15 = (f32[8,128]{1,0:T(8,128)S(1)}, f32[8,128]{1,0:T(8,128)S(1)}, u32[]{:S(2)}, u32[]{:S(2)}) collective-permute-start(f32[8,128]{1,0:T(8,128)S(1)} %add.127), channel_id=1, source_target_pairs={{0,8},{1,9},{2,10},{3,11},{4,12},{5,13},{6,14},{7,15},{8,0},{9,1},... | collective-permute-start | bytes 12296 | tf_op jit(solution)/shard_map/ppermute | solution.py:54
  221.4 3.6 %collective-permute-start.16 = (f32[8,128]{1,0:T(8,128)S(1)}, f32[8,128]{1,0:T(8,128)S(1)}, u32[]{:S(2)}, u32[]{:S(2)}) collective-permute-start(f32[8,128]{1,0:T(8,128)S(1)} %add.128), channel_id=1, source_target_pairs={{0,16},{1,17},{2,18},{3,19},{4,20},{5,21},{6,22},{7,23},{8,24},{9,... | collective-permute-start | bytes 12296 | tf_op jit(solution)/shard_map/ppermute | solution.py:54
  225.0 5.1 %collective-permute-start.17 = (f32[8,128]{1,0:T(8,128)S(1)}, f32[8,128]{1,0:T(8,128)S(1)}, u32[]{:S(2)}, u32[]{:S(2)}) collective-permute-start(f32[8,128]{1,0:T(8,128)S(1)} %add.129), channel_id=1, source_target_pairs={{0,32},{1,33},{2,34},{3,35},{4,36},{5,37},{6,38},{7,39},{8,40},{9,... | collective-permute-start | bytes 12296 | tf_op jit(solution)/shard_map/ppermute | solution.py:54
